TPU v7x, 256 devices: a whole 4x4x8 slice. The times are simulated.
256 devices in a mesh: seq: 32 (over x, z_lo, core), mp: 8 (over y, z_hi).
Axes of the slice: x: 4, y: 4, z: 8 (z_hi: 2, z_lo: 4; z = z_hi * 4 + z_lo), core: 2. Of those that a mesh axis runs over, the one named last changes fastest.
Arguments:
- tokens: bfloat16 [8192, 4096], P('seq', 'mp'), may hold values from -6 to 6
- norm_gain: bfloat16 [4096], replicated, may hold values from 0.5 to 1.5
- norm_bias: bfloat16 [4096], replicated, may hold values from -4 to 4
- w_query: bfloat16 [4096, 2048], P(None, 'mp'), may hold values from -0.25 to 0.25
- w_keyval: bfloat16 [4096, 2, 2048], P(None, None, 'mp'), may hold values from -0.09375 to 0.09375
- w_out: bfloat16 [2048, 4096], P('mp'), may hold values from -0.125 to 0.125
- prefix_key: bfloat16 [8192, 2048], P('seq', 'mp'), may hold values from -82 to 82
- prefix_value: bfloat16 [8192, 2048], P('seq', 'mp'), may hold values from -6 to 6
- lengths: int32 [16], replicated, may hold values from 1 to 1024, 8192 in all
- context: int32 [16], replicated, may hold values from 256 to 8192
- prefix_place: int32 [64], replicated, may hold values from 0 to 63, each once
Outputs:
- attn_out: bfloat16 [8192, 4096], P(('seq', 'mp'))
Inputs may be any that keep to these rules, and one draw needn't show every extreme that they name: The lengths add up to 8192, and one request has exactly 1024 tokens. Stored block j holds the prefix positions prefix_place[j] * 128 to prefix_place[j] * 128 + 127; every block appears once.
All inputs are finite; a program needn't handle non-finite values.
Results may differ from a plain program's by a relative error of at most 0.02.
The roundings to bfloat16 on the way count: a program that leaves them out, or rounds other values in their place, can miss the bound.
Values may be sent and summed in bfloat16 or wider, within the bound.
No kernel may reach another device: no remote copies, remote signals or barrier semaphores. Data moves between devices by JAX's collectives and lax.ppermute only.
A program may use at most 128 MiB of HBM per device.

v0:
```python
import math
import jax
import jax.numpy as jnp
from jax import lax
from jax.sharding import PartitionSpec as P

HD = 128
PBLOCK = 128
NEG_FILL = -1e30


def layer_norm(rows_in, norm_gain, norm_bias):
    as_float = rows_in.astype(jnp.float32)
    row_mean = jnp.mean(as_float, -1, keepdims=True)
    centered = as_float - row_mean
    row_var = jnp.mean(centered * centered, -1, keepdims=True)
    scaled = centered * lax.rsqrt(row_var + 1e-05)
    return (scaled * norm_gain.astype(jnp.float32) + norm_bias.astype(jnp.float32)).astype(
        jnp.bfloat16
    )


def rotate(column_block, position):
    head_dim = column_block.shape[-1]
    half_rot = head_dim // 8
    inverse_freq = jnp.power(
        jnp.float32(10000.0), -jnp.arange(half_rot, dtype=jnp.float32) * (8.0 / head_dim)
    )
    angles = position.astype(jnp.float32)[:, None] * inverse_freq[None, :]
    cosine = jnp.cos(angles)[:, None, :]
    sines = jnp.sin(angles)[:, None, :]
    first_half = column_block[..., :half_rot]
    second = column_block[..., half_rot : 2 * half_rot]
    return jnp.concatenate(
        [
            first_half * cosine - second * sines,
            second * cosine + first_half * sines,
            column_block[..., 2 * half_rot :],
        ],
        -1,
    )


def request_info(global_index, lengths, context):
    request_end = jnp.cumsum(lengths)
    starts = request_end - lengths
    inside = (
        (global_index[:, None] >= starts[None, :]) & (global_index[:, None] < request_end[None, :])
    ).astype(jnp.int32)
    labels = jnp.arange(lengths.shape[0], dtype=jnp.int32) + 1
    request = jnp.sum(inside * labels[None, :], 1) - 1
    cached_len = jnp.sum(inside * context[None, :], 1)
    position = jnp.sum(inside * (context - starts)[None, :], 1) + global_index
    return (request, cached_len, position)


def masked_softmax_attention(queries, key_sets, value_sets, visible_sets):
    scale = 1.0 / math.sqrt(queries.shape[-1])
    score_sets = [
        jnp.einsum("qhd,khd->hqk", queries, keys, preferred_element_type=jnp.float32) * scale
        for keys in key_sets
    ]
    row_max = None
    for scores, visible in zip(score_sets, visible_sets):
        part = jnp.max(jnp.where(visible[None], scores, NEG_FILL), -1)
        row_max = part if row_max is None else jnp.maximum(row_max, part)
    row_sum = 0.0
    weighted = 0.0
    for scores, visible, values in zip(score_sets, visible_sets, value_sets):
        probs = jnp.where(visible[None], jnp.exp(scores - row_max[..., None]), 0.0)
        row_sum = row_sum + jnp.sum(probs, -1)
        weighted = weighted + jnp.einsum(
            "hqk,khd->hqd", probs.astype(jnp.bfloat16), values, preferred_element_type=jnp.float32
        )
    return weighted / row_sum[..., None]


SUFFIX_SHARDS = 5


def body(
    tokens,
    norm_gain,
    norm_bias,
    w_query,
    w_keyval,
    w_out,
    prefix_key,
    prefix_value,
    lengths,
    context,
    prefix_place,
):
    prefix_rows = prefix_key.shape[0]
    local_heads = w_query.shape[1] // HD
    prefix_both = lax.all_gather(
        jnp.stack([prefix_key, prefix_value], 0), "seq", axis=1, tiled=True
    )
    gathered = lax.all_gather(tokens, "mp", axis=1, tiled=True)
    token_count = gathered.shape[0]
    feature_count = gathered.shape[1]
    normed = layer_norm(gathered, norm_gain, norm_bias)
    seq_index = lax.axis_index("seq")
    seq_count = lax.psum(1, "seq")
    global_index = seq_index * token_count + jnp.arange(token_count, dtype=jnp.int32)
    request, cached_len, position = request_info(global_index, lengths, context)
    query_raw = jnp.dot(normed, w_query, preferred_element_type=jnp.float32).reshape(
        token_count, local_heads, HD
    )
    key_value_raw = jnp.dot(
        normed, w_keyval.reshape(feature_count, -1), preferred_element_type=jnp.float32
    ).reshape(token_count, 2, local_heads, HD)
    queries = rotate(query_raw, position).astype(jnp.bfloat16)
    own_keys = rotate(key_value_raw[:, 0], position).astype(jnp.bfloat16)
    own_values = key_value_raw[:, 1].astype(jnp.bfloat16)
    key_value = jnp.stack([own_keys, own_values], 0)
    window = [key_value]
    for shift in range(1, SUFFIX_SHARDS):
        pairs = [(i, i + shift) for i in range(seq_count - shift)]
        window.insert(0, lax.ppermute(key_value, "seq", pairs))
    window = jnp.concatenate(window, 1)
    window_count = window.shape[1]
    key_index = (seq_index - (SUFFIX_SHARDS - 1)) * token_count + jnp.arange(
        window_count, dtype=jnp.int32
    )
    key_request = request_info(key_index, lengths, context)[0]
    sees_suffix = (
        (key_index[None, :] >= 0)
        & (key_request[None, :] == request[:, None])
        & (key_index[None, :] <= global_index[:, None])
    )
    prefix_all = prefix_both.shape[1]
    prefix_position = (
        prefix_place[:, None] * PBLOCK + jnp.arange(PBLOCK, dtype=jnp.int32)[None, :]
    ).reshape(-1)
    sees_prefix = prefix_position[None, :] < cached_len[:, None]
    prefix_keys = prefix_both[0].reshape(prefix_all, local_heads, HD)
    prefix_values = prefix_both[1].reshape(prefix_all, local_heads, HD)
    attended = masked_softmax_attention(
        queries, (prefix_keys, window[0]), (prefix_values, window[1]), (sees_prefix, sees_suffix)
    )
    heads_out = (
        attended.astype(jnp.bfloat16).transpose(1, 0, 2).reshape(token_count, local_heads * HD)
    )
    summed = lax.psum_scatter(
        jnp.dot(heads_out, w_out, preferred_element_type=jnp.float32).astype(jnp.bfloat16),
        "mp",
        scatter_dimension=0,
        tiled=True,
    )
    return summed


def solution(mesh):
    return jax.shard_map(
        body,
        mesh=mesh,
        in_specs=(
            P("seq", "mp"),
            P(),
            P(),
            P(None, "mp"),
            P(None, None, "mp"),
            P("mp", None),
            P("seq", "mp"),
            P("seq", "mp"),
            P(),
            P(),
            P(),
        ),
        out_specs=P(("seq", "mp"), None),
        check_vma=False,
    )
```

profile of v0, /device:TPU:2, one launch (start us, length us, event | category | flops | bytes accessed | tf_op | source)
XLA Modules:
  0.0 328.7 jit_solution(272534547121617955)
XLA Ops:
  6.5 0.7 all-gather.3.cloned.1.call-update
  7.3 1.0 copy.50
  8.3 1.0 copy.49
  9.3 0.7 pad_maximum_fusion
  10.1 0.7 copy.43
  10.9 0.1 reduce
  11.0 0.7 convert_element_type.57
  11.7 0.7 convert_element_type.56
  12.4 4.9 %copy.63 = bf16[512,8,2,256]{3,1,2,0:T(8,128)(2,1)} copy(bf16[512,8,2,256]{3,2,1,0:T(2,128)(2,1)} %bitcast.52) | data formatting | bytes 8388608
  17.3 6.4 %copy.52 = bf16[512,4096]{1,0:T(8,128)(2,1)} copy(bf16[512,4096]{0,1:T(8,128)(2,1)} %bitcast.51) | data formatting | bytes 8388608 | tf_op jit(solution)/shard_map/dot_general | solution.py:110
  23.9 0.1 multiply_cosine_fusion
  24.1 0.1 copy.47
  24.5 2.6 broadcast_compare_fusion
  27.1 61.3 %all-gather.3.cloned.1.call-done = bf16[256,4096]{1,0:T(8,128)(2,1)} async-done(((bf16[256,512]{1,0:T(8,128)(2,1)}), bf16[256,4096]{1,0:T(8,128)(2,1)}) %all-gather.3.cloned.1.call-update) | async-done | bytes 2097168 | tf_op jit(solution)/shard_map/all_gather | solution.py:99
  88.4 2.1 convert_reduce_fusion
  90.5 2.3 fusion.7
  92.8 1.4 fusion.41
  94.3 0.1 copy.60
  94.4 0.1 copy.61
  94.5 4.1 %fusion.13 = f32[256,2,2,128]{3,0,2,1:T(8,128)S(1)} fusion(bf16[2,2,128,4096]{3,2,1,0:T(8,128)(2,1)} %bitcast.53, bf16[256,4096]{1,0:T(8,128)(2,1)} %all-gather.3.cloned.1.call-done, f32[4096]{0:T(1024)S(1)} %convert_element_type.57, f32[4096]{0:T(1024)S(1)} %convert_element_type.56, f32[256]{0:T(256)S(1)} %add_rsqrt_fusion, f32[256]{0:T(256)S(1)} %broadcast_multiply_fusion), kind=kOutput, calls=%fused_computation.21 | convolution fusion | flops 1080033280 | bytes 6850560 | tf_op jit(solution)/shard_map/dot_general | solution.py:110
  98.8 0.9 fusion.32
  99.7 0.1 pad_maximum_fusion.1
  99.9 2.8 collective-permute-start
  102.7 1.9 collective-permute-start.1
  104.6 3.6 %collective-permute-start.2 = (bf16[2,256,2,128]{3,1,2,0:T(8,128)(2,1)S(1)}, bf16[2,256,2,128]{3,1,2,0:T(8,128)(2,1)}, u32[]{:S(2)}, u32[]{:S(2)}) collective-permute-start(bf16[2,256,2,128]{3,1,2,0:T(8,128)(2,1)S(1)} %pad_maximum_fusion.1), channel_id=1, source_target_pairs={{0,16},{8,24},{16,32},{24,40},{32,48},{40,56},{48,64},{56,72},{64,... | collective-permute-start | bytes 786440 | tf_op jit(solution)/shard_map/ppermute | solution.py:120
  108.2 0.4 compare_and_fusion
  108.7 0.9 slice.53
  109.6 4.3 %collective-permute-start.3 = (bf16[2,256,2,128]{3,1,2,0:T(8,128)(2,1)S(1)}, bf16[2,256,2,128]{3,1,2,0:T(8,128)(2,1)}, u32[]{:S(2)}, u32[]{:S(2)}) collective-permute-start(bf16[2,256,2,128]{3,1,2,0:T(8,128)(2,1)S(1)} %pad_maximum_fusion.1), channel_id=1, source_target_pairs={{0,8},{8,16},{16,24},{24,32},{32,40},{40,48},{48,56},{56,64},{64,7... | collective-permute-start | bytes 786440 | tf_op jit(solution)/shard_map/ppermute | solution.py:120
  113.9 0.7 copy.62
  114.6 22.2 %collective-permute-done = bf16[2,256,2,128]{3,1,2,0:T(8,128)(2,1)} collective-permute-done((bf16[2,256,2,128]{3,1,2,0:T(8,128)(2,1)S(1)}, bf16[2,256,2,128]{3,1,2,0:T(8,128)(2,1)}, u32[]{:S(2)}, u32[]{:S(2)}) %collective-permute-start) | collective-permute-done | bytes 262176 | tf_op jit(solution)/shard_map/ppermute | solution.py:120
  136.8 1.0 constant_dynamic-update-slice_fusion.4
  137.8 2.9 collective-permute-done.1
  140.7 1.0 constant_dynamic-update-slice_fusion.3
  141.7 1.0 constant_dynamic-update-slice_fusion.2
  142.7 1.0 constant_dynamic-update-slice_fusion.1
  143.7 0.2 constant_dynamic-update-slice_fusion
  143.9 1.0 copy-done.9
  145.0 3.3 select_reduce_fusion.1
  148.3 45.9 %all-gather.5.cloned.1.call-done = bf16[2,8192,256]{1,2,0:T(8,128)(2,1)} async-done(((bf16[2,256,256]{1,2,0:T(8,128)(2,1)}), bf16[2,8192,256]{1,2,0:T(8,128)(2,1)}) %all-gather.5.cloned.1.call-update) | async-done | bytes 8388624 | tf_op jit(solution)/shard_map/all_gather | solution.py:96
  194.1 6.0 %fusion.44 = (bf16[1,8192,256]{1,2,0:T(8,128)(2,1)}, bf16[1,8192,256]{1,2,0:T(8,128)(2,1)}) fusion(bf16[2,8192,256]{1,2,0:T(8,128)(2,1)} %all-gather.5.cloned.1.call-done), kind=kLoop, calls=%fused_computation.79 | loop fusion | bytes 16777216 | tf_op jit(solution)/shard_map/slice | solution.py:137
  200.2 6.4 %select_reduce_fusion = (f32[2,256]{1,0:T(2,128)S(1)}, f32[2,256,8192]{2,1,0:T(8,128)S(1)}) fusion(pred[256,8192]{1,0:T(8,128)(4,1)S(1)} %copy-done.2, bf16[8192,2,128]{0,2,1:T(8,128)(2,1)} %bitcast.55, bf16[256,2,96]{2,0,1:T(8,128)(2,1)S(1)} %copy-done.7, bf16[256,2,16]{2,0,1:T(8,128)(2,1)S(1)} %copy-done.5, bf16[256,2,16]{2,0,1:T(8,128)(2,1)S(1)} %copy-done.6), kind=kOutput, calls=%fused_computation.1 | convolution fusion | flops 1086717440 | bytes 23201792 | tf_op jit(solution)/shard_map/qhd,khd->hqk/dot_general | solution.py:60
  206.7 4.8 %fusion = f32[2,256]{1,0:T(2,128)S(1)} fusion(f32[2,256,8192]{2,1,0:T(8,128)S(1)} %get-tuple-element.23, f32[2,256]{1,0:T(2,128)S(1)} %max.7, pred[256,8192]{1,0:T(8,128)(4,1)S(1)} %copy-done.2), kind=kLoop, calls=%fused_computation.2 | loop fusion | flops 16776704 | bytes 18878464 | tf_op jit(solution)/shard_map/reduce_sum | solution.py:71
  211.4 0.9 copy-done.1
  212.4 9.4 %fusion.2 = f32[2,256,128]{1,2,0:T(8,128)S(1)} fusion(bf16[8192,2,128]{0,2,1:T(8,128)(2,1)} %bitcast.54, f32[2,256,8192]{2,1,0:T(8,128)} %copy-done.1, f32[2,256]{1,0:T(2,128)S(1)} %max.7, pred[256,8192]{1,0:T(8,128)(4,1)S(1)} %copy-done.2), kind=kOutput, calls=%fused_computation.4 | convolution fusion | flops 1090519040 | bytes 23332864 | tf_op jit(solution)/shard_map/hqk,khd->hqd/dot_general | solution.py:72
  221.8 0.8 fusion.11
  222.6 0.8 fusion.29
  223.4 2.1 convolution_convert_fusion
  225.5 96.6 %reduce-scatter.2.cloned.1.call-done = bf16[32,4096]{1,0:T(8,128)(2,1)} async-done(((bf16[256,4096]{1,0:T(8,128)(2,1)}), bf16[32,4096]{1,0:T(8,128)(2,1)}) %reduce-scatter.2.cloned.1.call-update) | async-done | bytes 262160 | tf_op jit(solution)/shard_map/reduce_scatter | solution.py:145
  (57 shorter events, 0.8 us)
Async XLA Ops:
  6.5 216.9 %copy-start = (bf16[256,4096]{1,0:T(8,128)(2,1)S(1)}, bf16[256,4096]{1,0:T(8,128)(2,1)}, u32[]{:S(2)}) copy-start(bf16[256,4096]{1,0:T(8,128)(2,1)} %param.16) | copy-start | bytes 6291460
  6.5 81.9 %all-gather.3.cloned.1.call-start = ((), (), s32[]{:S(2)}) async-start(), calls=%async_computation.1 | async-start | bytes 2359296 | tf_op jit(solution)/shard_map/all_gather | solution.py:99
  7.3 186.9 %all-gather.5.cloned.1.call-start = ((), (), s32[]{:S(2)}) async-start(), calls=%async_computation.2 | async-start | bytes 8650752 | tf_op jit(solution)/shard_map/all_gather | solution.py:96
  10.1 312.1 %reduce-scatter.2.cloned.1.call-start = ((), (), s32[]{:S(2)}) async-start(), calls=%async_computation.3 | async-start | bytes 2359296 | tf_op jit(solution)/shard_map/reduce_scatter | solution.py:145
  17.3 6.5 %copy-start.11 = (s32[16]{0:T(128)S(1)}, s32[16]{0:T(128)}, u32[]{:S(2)}) copy-start(s32[16]{0:T(128)} %param.19) | copy-start | bytes 196
  17.3 6.5 %copy-start.12 = (s32[16]{0:T(128)S(1)}, s32[16]{0:T(128)}, u32[]{:S(2)}) copy-start(s32[16]{0:T(128)} %param.20) | copy-start | bytes 196
  17.3 7.1 %copy-start.14 = (s32[64]{0:T(128)S(1)}, s32[64]{0:T(128)}, u32[]{:S(2)}) copy-start(s32[64]{0:T(128)} %param.21) | copy-start | bytes 772
  88.4 4.4 %copy-start.3 = (bf16[256,4096]{1,0:T(8,128)(2,1)S(1)}, bf16[256,4096]{1,0:T(8,128)(2,1)}, u32[]{:S(2)}) copy-start(bf16[256,4096]{1,0:T(8,128)(2,1)} %all-gather.3.cloned.1.call-done) | copy-start | bytes 6291460
  88.4 4.4 %copy-start.13 = (bf16[4096,256]{1,0:T(8,128)(2,1)S(1)}, bf16[4096,256]{1,0:T(8,128)(2,1)}, u32[]{:S(2)}) copy-start(bf16[4096,256]{1,0:T(8,128)(2,1)} %param.14) | copy-start | bytes 6291460
  94.3 4.4 %copy-start.8 = (f32[256,256]{0,1:T(8,128)}, f32[256,256]{0,1:T(8,128)S(1)}, u32[]{:S(2)}) copy-start(f32[256,256]{0,1:T(8,128)S(1)} %fusion.41) | copy-start | bytes 786436
  99.7 45.2 %copy-start.5 = (bf16[256,2,16]{2,0,1:T(8,128)(2,1)S(1)}, bf16[256,2,16]{2,0,1:T(8,128)(2,1)}, u32[]{:S(2)}) copy-start(bf16[256,2,16]{2,0,1:T(8,128)(2,1)} %get-tuple-element.16) | copy-start | bytes 49156
  99.9 36.9 %collective-permute-start = (bf16[2,256,2,128]{3,1,2,0:T(8,128)(2,1)S(1)}, bf16[2,256,2,128]{3,1,2,0:T(8,128)(2,1)}, u32[]{:S(2)}, u32[]{:S(2)}) collective-permute-start(bf16[2,256,2,128]{3,1,2,0:T(8,128)(2,1)S(1)} %pad_maximum_fusion.1), channel_id=1, source_target_pairs={{0,32},{8,40},{16,48},{24,56},{32,64},{40,72},{48,80},{56,88},{64,... | collective-permute-start | bytes 786440 | tf_op jit(solution)/shard_map/ppermute | solution.py:120
  102.7 38.0 %collective-permute-start.1 = (bf16[2,256,2,128]{3,1,2,0:T(8,128)(2,1)S(1)}, bf16[2,256,2,128]{3,1,2,0:T(8,128)(2,1)}, u32[]{:S(2)}, u32[]{:S(2)}) collective-permute-start(bf16[2,256,2,128]{3,1,2,0:T(8,128)(2,1)S(1)} %pad_maximum_fusion.1), channel_id=1, source_target_pairs={{0,24},{8,32},{16,40},{24,48},{32,56},{40,64},{48,72},{56,80},{64,... | collective-permute-start | bytes 786440 | tf_op jit(solution)/shard_map/ppermute | solution.py:120
  104.6 37.1 %collective-permute-start.2 = (bf16[2,256,2,128]{3,1,2,0:T(8,128)(2,1)S(1)}, bf16[2,256,2,128]{3,1,2,0:T(8,128)(2,1)}, u32[]{:S(2)}, u32[]{:S(2)}) collective-permute-start(bf16[2,256,2,128]{3,1,2,0:T(8,128)(2,1)S(1)} %pad_maximum_fusion.1), channel_id=1, source_target_pairs={{0,16},{8,24},{16,32},{24,40},{32,48},{40,56},{48,64},{56,72},{64,... | collective-permute-start | bytes 786440 | tf_op jit(solution)/shard_map/ppermute | solution.py:120
  109.6 33.1 %collective-permute-start.3 = (bf16[2,256,2,128]{3,1,2,0:T(8,128)(2,1)S(1)}, bf16[2,256,2,128]{3,1,2,0:T(8,128)(2,1)}, u32[]{:S(2)}, u32[]{:S(2)}) collective-permute-start(bf16[2,256,2,128]{3,1,2,0:T(8,128)(2,1)S(1)} %pad_maximum_fusion.1), channel_id=1, source_target_pairs={{0,8},{8,16},{16,24},{24,32},{32,40},{40,48},{48,56},{56,64},{64,7... | collective-permute-start | bytes 786440 | tf_op jit(solution)/shard_map/ppermute | solution.py:120
  143.9 1.1 copy-start.9
  148.3 51.9 %copy-start.6 = (bf16[256,2,16]{2,0,1:T(8,128)(2,1)S(1)}, bf16[256,2,16]{2,0,1:T(8,128)(2,1)}, u32[]{:S(2)}) copy-start(bf16[256,2,16]{2,0,1:T(8,128)(2,1)} %get-tuple-element.17) | copy-start | bytes 49156
  148.3 51.9 %copy-start.7 = (bf16[256,2,96]{2,0,1:T(8,128)(2,1)S(1)}, bf16[256,2,96]{2,0,1:T(8,128)(2,1)}, u32[]{:S(2)}) copy-start(bf16[256,2,96]{2,0,1:T(8,128)(2,1)} %copy.62) | copy-start | bytes 294916
  194.1 6.0 %copy-start.2 = (pred[256,8192]{1,0:T(8,128)(4,1)S(1)}, pred[256,8192]{1,0:T(8,128)(4,1)}, u32[]{:S(2)}) copy-start(pred[256,8192]{1,0:T(8,128)(4,1)} %broadcast_compare_fusion) | copy-start | bytes 6291460
  206.6 5.7 %copy-start.1 = (f32[2,256,8192]{2,1,0:T(8,128)}, f32[2,256,8192]{2,1,0:T(8,128)S(1)}, u32[]{:S(2)}) copy-start(f32[2,256,8192]{2,1,0:T(8,128)S(1)} %get-tuple-element.23) | copy-start | bytes 50331652
  212.3 9.5 %copy-start.4 = (f32[2,256,1280]{2,1,0:T(8,128)S(1)}, f32[2,256,1280]{2,1,0:T(8,128)}, u32[]{:S(2)}) copy-start(f32[2,256,1280]{2,1,0:T(8,128)} %get-tuple-element.25) | copy-start | bytes 7864324
  212.3 10.3 %copy-start.10 = (bf16[2,1280,2,128]{3,1,2,0:T(8,128)(2,1)S(1)}, bf16[2,1280,2,128]{3,1,2,0:T(8,128)(2,1)}, u32[]{:S(2)}) copy-start(bf16[2,1280,2,128]{3,1,2,0:T(8,128)(2,1)} %copy-done.9) | copy-start | bytes 3932164
Sparse Core Ops, SparseCore 0:
  9.8 78.5 all-gather.2
  90.2 103.9 all-gather.4
  225.7 96.4 reduce-scatter.1
where the time goes:
time: 329 us
  waiting for transfers between devices  230 us (70%)
  local copies, waits for them, and re-layouts  28.3 us (9%)
  matrix products  27.6 us (8%)
  other arithmetic  17 us (5%)
  between operations  13.5 us (4%)
  starting transfers between devices  12.7 us (4%)
    reduce_scatter x1, waiting for transfers between devices, body(): lax.psum_scatter(jnp.dot(heads_out, w_out, preferred_element_type=jnp.flo...  96.6 us
    all_gather x1, waiting for transfers between devices, body(): gathered = lax.all_gather(tokens, 'mp', axis=1, tiled=True)  61.3 us
    all_gather x1, waiting for transfers between devices, body(): lax.all_gather(jnp.stack([prefix_key, prefix_value], 0), 'seq', axis=1, t...  45.9 us
    ppermute x4, waiting for transfers between devices, body(): window.insert(0, lax.ppermute(key_value, 'seq', pairs))  25.1 us
    unnamed x40, local copies, waits for them, and re-layouts  13.8 us
    ppermute x4, starting transfers between devices, body(): window.insert(0, lax.ppermute(key_value, 'seq', pairs))  12.6 us
    dot_general x2, matrix products, masked_softmax_attention(): jnp.einsum('hqk,khd->hqd', probs.astype(jnp.bfloat16), values, preferred_...  10.2 us
    dot_general x2, matrix products, masked_softmax_attention(): jnp.einsum('qhd,khd->hqk', queries, keys, preferred_element_type=jnp.floa...  9.72 us
  transfers between devices with their start and end apart: 7, of which 5 were waited for; matrix products, arithmetic and copies ran while one was open for 12% of the time, Pallas kernels for 0%

commit v1 on v0

--- a/solution.py
+++ b/solution.py
@@ -7,6 +7,15 @@
 HD = 128
 PBLOCK = 128
 NEG_FILL = -1e30
+step_on_record_in = lambda mine_x, dim_no: jnp.concatenate(
+    jax.lax.all_to_all(
+        jnp.stack(jax.lax.axis_size("mp") * [mine_x], axis=0),
+        axis_name="mp",
+        split_axis=0,
+        concat_axis=0,
+    ),
+    axis=dim_no,
+)
 
 
 def layer_norm(rows_in, norm_gain, norm_bias):
@@ -96,7 +105,7 @@
     prefix_both = lax.all_gather(
         jnp.stack([prefix_key, prefix_value], 0), "seq", axis=1, tiled=True
     )
-    gathered = lax.all_gather(tokens, "mp", axis=1, tiled=True)
+    gathered = step_on_record_in(tokens, 1)
     token_count = gathered.shape[0]
     feature_count = gathered.shape[1]
     normed = layer_norm(gathered, norm_gain, norm_bias)

time: 329 us -> 298 us (0.906)
  waiting for transfers between devices: 230 us -> 188 us
  starting transfers between devices: 12.7 us -> 24.3 us
  local copies, waits for them, and re-layouts: 28.3 us -> 34 us
  matrix products: 27.6 us -> 22.6 us
    all_gather x1 -> x0, waiting for transfers between devices: 61.3 us -> none  [body(): gathered = lax.all_gather(tokens, 'mp', axis=1, tiled=True)]
    all_to_all x0 -> x1, waiting for transfers between devices: none -> 33.8 us  [jax.lax.all_to_all(jnp.stack(jax.lax.axis_size('mp') * [mine_x], axis=0),...]
    all_gather x1, waiting for transfers between devices: 45.9 us -> 12.5 us  [body(): lax.all_gather(jnp.stack([prefix_key, prefix_value], 0), 'seq', axis=1, t...]
    ppermute x4, waiting for transfers between devices: 25.1 us -> 44.3 us  [body(): window.insert(0, lax.ppermute(key_value, 'seq', pairs))]
    all_to_all x0 -> x1, starting transfers between devices: none -> 11.2 us  [jax.lax.all_to_all(jnp.stack(jax.lax.axis_size('mp') * [mine_x], axis=0),...]
    dot_general x0 -> x1, local copies, waits for them, and re-layouts: none -> 4.21 us  [body(): jnp.dot(normed, w_query, preferred_element_type=jnp.float32)]
    all_to_all x0 -> x1, local copies, waits for them, and re-layouts: none -> 3.91 us  [jax.lax.all_to_all(jnp.stack(jax.lax.axis_size('mp') * [mine_x], axis=0),...]
    unnamed x40 -> x35, local copies, waits for them, and re-layouts: 13.8 us -> 10.8 us
where the time goes in v1:
time: 298 us; the launch traced here: 297 us
  waiting for transfers between devices  188 us (63%)
  local copies, waits for them, and re-layouts  34 us (11%)
  starting transfers between devices  24.3 us (8%)
  matrix products  22.6 us (8%)
  other arithmetic  14.3 us (5%)
  between operations  13.8 us (5%)
    reduce_scatter x1, waiting for transfers between devices, body(): lax.psum_scatter(jnp.dot(heads_out, w_out, preferred_element_type=jnp.flo...  97.5 us
    ppermute x4, waiting for transfers between devices, body(): window.insert(0, lax.ppermute(key_value, 'seq', pairs))  44.3 us
    all_to_all x1, waiting for transfers between devices, jax.lax.all_to_all(jnp.stack(jax.lax.axis_size('mp') * [mine_x], axis=0),...  33.8 us
    ppermute x4, starting transfers between devices, body(): window.insert(0, lax.ppermute(key_value, 'seq', pairs))  13.1 us
    all_gather x1, waiting for transfers between devices, body(): lax.all_gather(jnp.stack([prefix_key, prefix_value], 0), 'seq', axis=1, t...  12.5 us
    all_to_all x1, starting transfers between devices, jax.lax.all_to_all(jnp.stack(jax.lax.axis_size('mp') * [mine_x], axis=0),...  11.2 us
    unnamed x35, local copies, waits for them, and re-layouts  10.8 us
    dot_general x2, matrix products, masked_softmax_attention(): jnp.einsum('hqk,khd->hqd', probs.astype(jnp.bfloat16), values, preferred_...  10.2 us
  transfers between devices with their start and end apart: 7, of which 5 were waited for; matrix products, arithmetic and copies ran while one was open for 12% of the time, Pallas kernels for 0%

profile of v1, /device:TPU:2, one launch (start us, length us, event | category | flops | bytes accessed | tf_op | source)
XLA Modules:
  0.0 297.1 jit_solution(17618882373564458748)
XLA Ops:
  6.5 1.1 copy.54
  7.7 1.0 copy.53
  8.7 0.7 pad_maximum_fusion
  9.4 0.0 all-gather.2.cloned.1.call-update
  9.5 2.5 stack.10
  11.9 11.2 %all-to-all-start = ((bf16[8,256,512]{2,1,0:T(8,128)(2,1)}), bf16[8,256,512]{2,1,0:T(8,128)(2,1)}, u32[]{:S(2)}, u32[]{:S(2)}) async-start(bf16[8,256,512]{2,1,0:T(8,128)(2,1)} %stack.10), calls=%async_computation | async-start | bytes 4194304 | tf_op jit(solution)/shard_map/all_to_all | solution.py:11
  23.2 0.0 reduce-scatter.2.cloned.1.call-start
  23.3 0.1 copy.49
  23.4 0.1 reduce.4
  23.6 4.2 %copy.68 = bf16[256,4096]{1,0:T(8,128)(2,1)} copy(bf16[256,4096]{0,1:T(8,128)(2,1)} %bitcast.64) | data formatting | bytes 4194304 | tf_op jit(solution)/shard_map/dot_general | solution.py:116
  27.8 4.9 %copy.70 = bf16[512,8,2,256]{3,1,2,0:T(8,128)(2,1)} copy(bf16[512,8,2,256]{3,2,1,0:T(2,128)(2,1)} %bitcast.60) | data formatting | bytes 8388608
  32.7 6.4 %copy.57 = bf16[512,4096]{1,0:T(8,128)(2,1)} copy(bf16[512,4096]{0,1:T(8,128)(2,1)} %bitcast.56) | data formatting | bytes 8388608 | tf_op jit(solution)/shard_map/dot_general | solution.py:119
  39.2 0.1 select_reduce_fusion.2
  39.3 0.1 select_reduce_fusion.3
  39.4 0.1 add_bitcast_fusion
  39.5 0.1 multiply_cosine_fusion
  39.6 2.6 broadcast_compare_fusion
  42.2 33.8 %all-to-all-done = bf16[8,256,512]{2,1,0:T(8,128)(2,1)} async-done(((bf16[8,256,512]{2,1,0:T(8,128)(2,1)}), bf16[8,256,512]{2,1,0:T(8,128)(2,1)}, u32[]{:S(2)}, u32[]{:S(2)}) %all-to-all-start) | async-done | bytes 2097184 | tf_op jit(solution)/shard_map/all_to_all | solution.py:11
  76.0 3.9 %copy.50 = bf16[8,256,512]{1,2,0:T(8,128)(2,1)} copy(bf16[8,256,512]{2,1,0:T(8,128)(2,1)} %all-to-all-done) | data formatting | bytes 4194304 | tf_op jit(solution)/shard_map/all_to_all | solution.py:11
  80.0 2.3 convert_reduce_fusion
  82.3 0.6 fusion.7
  82.9 1.4 fusion.10
  84.3 0.8 copy-done.5
  85.1 1.2 fusion.43
  86.3 0.3 copy-done.4
  86.7 0.7 fusion.42
  87.5 4.0 %collective-permute-start = (bf16[2,256,2,128]{1,3,2,0:T(8,128)(2,1)S(1)}, bf16[2,256,2,128]{1,3,2,0:T(8,128)(2,1)S(1)}, u32[]{:S(2)}, u32[]{:S(2)}) collective-permute-start(bf16[2,256,2,128]{1,3,2,0:T(8,128)(2,1)S(1)} %pad_maximum_fusion.1), channel_id=1, source_target_pairs={{0,32},{8,40},{16,48},{24,56},{32,64},{40,72},{48,80},{56,88},{64,... | collective-permute-start | bytes 786440 | tf_op jit(solution)/shard_map/ppermute | solution.py:129
  91.5 1.9 collective-permute-start.1
  93.5 1.9 collective-permute-start.2
  95.4 0.4 compare_and_fusion
  95.8 5.2 %collective-permute-start.3 = (bf16[2,256,2,128]{1,3,2,0:T(8,128)(2,1)S(1)}, bf16[2,256,2,128]{1,3,2,0:T(8,128)(2,1)S(1)}, u32[]{:S(2)}, u32[]{:S(2)}) collective-permute-start(bf16[2,256,2,128]{1,3,2,0:T(8,128)(2,1)S(1)} %pad_maximum_fusion.1), channel_id=1, source_target_pairs={{0,8},{8,16},{16,24},{24,32},{32,40},{40,48},{48,56},{56,64},{64,7... | collective-permute-start | bytes 786440 | tf_op jit(solution)/shard_map/ppermute | solution.py:129
  101.0 27.7 %collective-permute-done = bf16[2,256,2,128]{1,3,2,0:T(8,128)(2,1)S(1)} collective-permute-done((bf16[2,256,2,128]{1,3,2,0:T(8,128)(2,1)S(1)}, bf16[2,256,2,128]{1,3,2,0:T(8,128)(2,1)S(1)}, u32[]{:S(2)}, u32[]{:S(2)}) %collective-permute-start) | collective-permute-done | bytes 262176 | tf_op jit(solution)/shard_map/ppermute | solution.py:129
  128.8 16.6 %collective-permute-done.1 = bf16[2,256,2,128]{1,3,2,0:T(8,128)(2,1)S(1)} collective-permute-done((bf16[2,256,2,128]{1,3,2,0:T(8,128)(2,1)S(1)}, bf16[2,256,2,128]{1,3,2,0:T(8,128)(2,1)S(1)}, u32[]{:S(2)}, u32[]{:S(2)}) %collective-permute-start.1) | collective-permute-done | bytes 262176 | tf_op jit(solution)/shard_map/ppermute | solution.py:129
  145.5 0.0 collective-permute-done.3
  145.5 1.0 copy-done.7
  146.6 2.3 select_reduce_fusion.1
  148.9 12.5 %all-gather.2.cloned.1.call-done = bf16[2,8192,256]{1,2,0:T(8,128)(2,1)} async-done(((bf16[2,256,256]{1,2,0:T(8,128)(2,1)}), bf16[2,8192,256]{1,2,0:T(8,128)(2,1)}) %all-gather.2.cloned.1.call-update) | async-done | bytes 8388624 | tf_op jit(solution)/shard_map/all_gather | solution.py:105
  161.3 6.0 %fusion.41 = (bf16[1,8192,256]{1,2,0:T(8,128)(2,1)}, bf16[1,8192,256]{1,2,0:T(8,128)(2,1)}) fusion(bf16[2,8192,256]{1,2,0:T(8,128)(2,1)} %all-gather.2.cloned.1.call-done), kind=kLoop, calls=%fused_computation.79 | loop fusion | bytes 16777216 | tf_op jit(solution)/shard_map/slice | solution.py:146
  167.4 6.1 %select_reduce_fusion = (f32[2,256]{1,0:T(2,128)S(1)}, f32[2,256,8192]{2,1,0:T(8,128)S(1)}) fusion(pred[256,8192]{1,0:T(8,128)(4,1)S(1)} %copy-done.3, bf16[8192,2,128]{0,2,1:T(8,128)(2,1)} %bitcast.63, bf16[256,2,96]{0,2,1:T(8,128)(2,1)S(1)} %slice.91, bf16[256,2,16]{0,2,1:T(8,128)(2,1)S(1)} %get-tuple-element.16, bf16[256,2,16]{0,2,1:T(8,128)(2,1)S(1)} %get-tuple-element.17), kind=kOutput, calls=%fused_computation.1 | convolution fusion | flops 1086717440 | bytes 23201792 | tf_op jit(solution)/shard_map/qhd,khd->hqk/dot_general | solution.py:69
  173.5 4.8 %fusion = f32[2,256]{1,0:T(2,128)S(1)} fusion(f32[2,256,8192]{2,1,0:T(8,128)S(1)} %get-tuple-element.21, f32[2,256]{1,0:T(2,128)S(1)} %max.7, pred[256,8192]{1,0:T(8,128)(4,1)S(1)} %copy-done.3), kind=kLoop, calls=%fused_computation.2 | loop fusion | flops 16776704 | bytes 18878464 | tf_op jit(solution)/shard_map/reduce_sum | solution.py:80
  178.3 0.9 copy-done.2
  179.2 9.4 %fusion.2 = f32[2,256,128]{1,2,0:T(8,128)S(1)} fusion(bf16[8192,2,128]{0,2,1:T(8,128)(2,1)} %bitcast.62, f32[2,256,8192]{2,1,0:T(8,128)} %copy-done.2, f32[2,256]{1,0:T(2,128)S(1)} %max.7, pred[256,8192]{1,0:T(8,128)(4,1)S(1)} %copy-done.3), kind=kOutput, calls=%fused_computation.4 | convolution fusion | flops 1090519040 | bytes 23332864 | tf_op jit(solution)/shard_map/hqk,khd->hqd/dot_general | solution.py:81
  188.6 0.8 fusion.11
  189.4 0.5 copy-done.8
  189.9 0.7 fusion.27
  190.7 2.1 convolution_convert_fusion
  192.7 0.0 reduce-scatter.2.cloned.1.call-update
  192.8 97.5 %reduce-scatter.2.cloned.1.call-done = bf16[32,4096]{1,0:T(8,128)(2,1)} async-done(((bf16[256,4096]{1,0:T(8,128)(2,1)}), bf16[32,4096]{1,0:T(8,128)(2,1)}) %reduce-scatter.2.cloned.1.call-update) | async-done | bytes 262160 | tf_op jit(solution)/shard_map/reduce_scatter | solution.py:154
  (52 shorter events, 0.4 us)
Async XLA Ops:
  6.5 184.1 %copy-start = (bf16[256,4096]{1,0:T(8,128)(2,1)S(1)}, bf16[256,4096]{1,0:T(8,128)(2,1)}, u32[]{:S(2)}) copy-start(bf16[256,4096]{1,0:T(8,128)(2,1)} %param.16) | copy-start | bytes 6291460
  6.5 154.8 %all-gather.2.cloned.1.call-start = ((), (), s32[]{:S(2)}) async-start(), calls=%async_computation.2 | async-start | bytes 8650752 | tf_op jit(solution)/shard_map/all_gather | solution.py:105
  11.9 11.3 %copy-start.11 = (s32[16]{0:T(128)S(1)}, s32[16]{0:T(128)}, u32[]{:S(2)}) copy-start(s32[16]{0:T(128)} %param.19) | copy-start | bytes 196
  11.9 11.6 %copy-start.9 = (bf16[4096]{0:T(1024)(128)(2,1)S(1)}, bf16[4096]{0:T(1024)(128)(2,1)}, u32[]{:S(2)}) copy-start(bf16[4096]{0:T(1024)(128)(2,1)} %param.13) | copy-start | bytes 24580
  11.9 11.6 %copy-start.10 = (bf16[4096]{0:T(1024)(128)(2,1)S(1)}, bf16[4096]{0:T(1024)(128)(2,1)}, u32[]{:S(2)}) copy-start(bf16[4096]{0:T(1024)(128)(2,1)} %param.12) | copy-start | bytes 24580
  11.9 64.1 %all-to-all-start = ((bf16[8,256,512]{2,1,0:T(8,128)(2,1)}), bf16[8,256,512]{2,1,0:T(8,128)(2,1)}, u32[]{:S(2)}, u32[]{:S(2)}) async-start(bf16[8,256,512]{2,1,0:T(8,128)(2,1)} %stack.10), calls=%async_computation | async-start | bytes 4194304 | tf_op jit(solution)/shard_map/all_to_all | solution.py:11
  23.2 267.2 %reduce-scatter.2.cloned.1.call-start = ((), (), s32[]{:S(2)}) async-start(), calls=%async_computation.3 | async-start | bytes 2359296 | tf_op jit(solution)/shard_map/reduce_scatter | solution.py:154
  32.7 6.4 %copy-start.12 = (s32[16]{0:T(128)S(1)}, s32[16]{0:T(128)}, u32[]{:S(2)}) copy-start(s32[16]{0:T(128)} %param.20) | copy-start | bytes 196
  32.7 6.6 %copy-start.13 = (s32[64]{0:T(128)S(1)}, s32[64]{0:T(128)}, u32[]{:S(2)}) copy-start(s32[64]{0:T(128)} %param.21) | copy-start | bytes 772
  80.0 2.3 copy-start.1
  82.9 2.2 copy-start.5
  85.1 1.6 copy-start.4
  87.5 41.3 %collective-permute-start = (bf16[2,256,2,128]{1,3,2,0:T(8,128)(2,1)S(1)}, bf16[2,256,2,128]{1,3,2,0:T(8,128)(2,1)S(1)}, u32[]{:S(2)}, u32[]{:S(2)}) collective-permute-start(bf16[2,256,2,128]{1,3,2,0:T(8,128)(2,1)S(1)} %pad_maximum_fusion.1), channel_id=1, source_target_pairs={{0,32},{8,40},{16,48},{24,56},{32,64},{40,72},{48,80},{56,88},{64,... | collective-permute-start | bytes 786440 | tf_op jit(solution)/shard_map/ppermute | solution.py:129
  91.5 53.9 %collective-permute-start.1 = (bf16[2,256,2,128]{1,3,2,0:T(8,128)(2,1)S(1)}, bf16[2,256,2,128]{1,3,2,0:T(8,128)(2,1)S(1)}, u32[]{:S(2)}, u32[]{:S(2)}) collective-permute-start(bf16[2,256,2,128]{1,3,2,0:T(8,128)(2,1)S(1)} %pad_maximum_fusion.1), channel_id=1, source_target_pairs={{0,24},{8,32},{16,40},{24,48},{32,56},{40,64},{48,72},{56,80},{64,... | collective-permute-start | bytes 786440 | tf_op jit(solution)/shard_map/ppermute | solution.py:129
  93.5 52.0 %collective-permute-start.2 = (bf16[2,256,2,128]{1,3,2,0:T(8,128)(2,1)S(1)}, bf16[2,256,2,128]{1,3,2,0:T(8,128)(2,1)S(1)}, u32[]{:S(2)}, u32[]{:S(2)}) collective-permute-start(bf16[2,256,2,128]{1,3,2,0:T(8,128)(2,1)S(1)} %pad_maximum_fusion.1), channel_id=1, source_target_pairs={{0,16},{8,24},{16,32},{24,40},{32,48},{40,56},{48,64},{56,72},{64,... | collective-permute-start | bytes 786440 | tf_op jit(solution)/shard_map/ppermute | solution.py:129
  95.8 49.6 %collective-permute-start.3 = (bf16[2,256,2,128]{1,3,2,0:T(8,128)(2,1)S(1)}, bf16[2,256,2,128]{1,3,2,0:T(8,128)(2,1)S(1)}, u32[]{:S(2)}, u32[]{:S(2)}) collective-permute-start(bf16[2,256,2,128]{1,3,2,0:T(8,128)(2,1)S(1)} %pad_maximum_fusion.1), channel_id=1, source_target_pairs={{0,8},{8,16},{16,24},{24,32},{32,40},{40,48},{48,56},{56,64},{64,7... | collective-permute-start | bytes 786440 | tf_op jit(solution)/shard_map/ppermute | solution.py:129
  145.5 1.1 copy-start.7
  161.3 6.0 %copy-start.3 = (pred[256,8192]{1,0:T(8,128)(4,1)S(1)}, pred[256,8192]{1,0:T(8,128)(4,1)}, u32[]{:S(2)}) copy-start(pred[256,8192]{1,0:T(8,128)(4,1)} %broadcast_compare_fusion) | copy-start | bytes 6291460
  173.4 5.7 %copy-start.2 = (f32[2,256,8192]{2,1,0:T(8,128)}, f32[2,256,8192]{2,1,0:T(8,128)S(1)}, u32[]{:S(2)}) copy-start(f32[2,256,8192]{2,1,0:T(8,128)S(1)} %get-tuple-element.21) | copy-start | bytes 50331652
  179.2 9.5 %copy-start.6 = (f32[2,256,1280]{2,1,0:T(8,128)S(1)}, f32[2,256,1280]{2,1,0:T(8,128)}, u32[]{:S(2)}) copy-start(f32[2,256,1280]{2,1,0:T(8,128)} %get-tuple-element.23) | copy-start | bytes 7864324
  188.6 1.3 copy-start.8
Sparse Core Ops, SparseCore 0:
  9.6 151.6 all-gather.1
  192.9 97.3 reduce-scatter.1
